TPU v7x, 32 devices: a whole 2x2x4 slice. The times are simulated.
32 devices in a mesh: req: 2 (over x), tile: 16 (over z, y, core).
Axes of the slice: x: 2, y: 2, z: 4, core: 2. Of those that a mesh axis runs over, the one named last changes fastest.
Arguments:
- queries: bfloat16 [32, 512, 384], P(('req', 'tile')), parts along dimension 0, may hold values from -12 to 12
- keys: bfloat16 [32, 512, 384], P(('req', 'tile')), parts along dimension 0, may hold values from -5 to 5
- values: bfloat16 [32, 512, 384], P(('req', 'tile')), parts along dimension 0, may hold values from -6 to 6
- text_keys: bfloat16 [512, 1536], P(('req', 'tile')), parts along dimension 0, may hold values from -6 to 6
- text_values: bfloat16 [512, 1536], P(('req', 'tile')), parts along dimension 0, may hold values from -6 to 6
- text_mask: int32 [512], P(('req', 'tile')), parts along dimension 0, may hold values 0 or 1
Outputs:
- attended: bfloat16 [32, 512, 384], P(('req', 'tile')), parts along dimension 0
There are 2 independent parts, one for each index of `req`. A program takes and returns all parts, laid end to end along the dimension named above; each array names one. Nothing has to cross between parts.
All inputs are finite; a program needn't handle non-finite values. No bound on the sum of `text_mask` on one device may be relied on, other than what follows from the above.
Results may differ from a plain program's by a relative error of at most 0.004.
Values may be sent and summed in bfloat16 or wider, within the bound.
No kernel may reach another device: no remote copies, remote signals or barrier semaphores. Data moves between devices by JAX's collectives and lax.ppermute only.
A program may use at most 192 MiB of HBM per device.

v0:
```python
import math
import jax
import jax.numpy as jnp
from jax import lax
from jax.sharding import PartitionSpec as P

TS = 8
HEAD_DIM = 128
HEAD_GROUPS = 4
MASKED = -1e30


def passed_along(value, axis, steps):
    count = lax.axis_size(axis)
    first, last = (max(0, -steps), min(count, count - steps))
    return lax.ppermute(value, axis, [(source, source + steps) for source in range(first, last)])


def shortened(value):
    return jax.tree.map(lambda a: a.astype(jnp.bfloat16) if a.dtype == jnp.float32 else a, value)


def fold_block(running, query_heads, key_block, value_block, key_keep):
    row_top, row_total, summed = running
    head_count = query_heads.shape[1]
    key_heads = key_block.reshape(key_block.shape[0], head_count, HEAD_DIM)
    value_heads = value_block.reshape(value_block.shape[0], head_count, HEAD_DIM)
    scores = jnp.einsum("qhd,khd->hqk", query_heads, key_heads, preferred_element_type=jnp.float32)
    scores = scores * (1.0 / math.sqrt(HEAD_DIM))
    scores = jnp.where(key_keep[None, None, :], scores, MASKED)
    new_top = jnp.maximum(row_top, jnp.max(scores, axis=-1))
    scale_down = jnp.exp(row_top - new_top)
    exp_terms = jnp.where(key_keep[None, None, :], jnp.exp(scores - new_top[:, :, None]), 0.0)
    row_total = row_total * scale_down + jnp.sum(exp_terms, axis=-1)
    weights = exp_terms.astype(jnp.bfloat16)
    summed = summed * scale_down[:, :, None] + jnp.einsum(
        "hqk,khd->hqd", weights, value_heads, preferred_element_type=jnp.float32
    )
    return (new_top, row_total, summed)


def shards(queries, keys, values, text_keys, text_values, text_mask):
    tokens = queries.shape[1]
    lane_width = queries.shape[2]
    head_count = lane_width // HEAD_DIM
    query_heads = queries[0].reshape(tokens, head_count, HEAD_DIM)
    own_pair = jnp.stack([keys[0], values[0]])
    group_count = HEAD_GROUPS
    tiles_all = lax.axis_size("tile") // group_count
    grid_w = min(4, tiles_all)
    grid_h = min(4, tiles_all // grid_w)
    grid_f = tiles_all // (grid_w * grid_h)
    frames_valid = grid_f * TS - TS // 4
    my_index = lax.axis_index("tile")
    tile_id = my_index // group_count
    head_group = my_index % group_count
    w_pos = tile_id % grid_w
    h_pos = tile_id // grid_w % grid_h
    f_pos = tile_id // (grid_w * grid_h)
    local_frame = jnp.arange(tokens, dtype=jnp.int32) // (TS * TS)

    def keep_mask(off_frame, off_height, off_width):
        inside = (
            (f_pos + off_frame >= 0)
            & (f_pos + off_frame < grid_f)
            & (h_pos + off_height >= 0)
            & (h_pos + off_height < grid_h)
            & (w_pos + off_width >= 0)
            & (w_pos + off_width < grid_w)
        )
        return inside & ((f_pos + off_frame) * TS + local_frame < frames_valid)

    running = (
        jnp.full((head_count, tokens), MASKED, jnp.float32),
        jnp.zeros((head_count, tokens), jnp.float32),
        jnp.zeros((head_count, tokens, HEAD_DIM), jnp.float32),
    )
    text_flags = text_mask.astype(jnp.bfloat16)
    piece_keys = lax.dynamic_slice_in_dim(
        lax.all_gather(text_keys, "tile", axis=0, tiled=True),
        head_group * lane_width,
        lane_width,
        1,
    )
    piece_values = lax.dynamic_slice_in_dim(
        lax.all_gather(text_values, "tile", axis=0, tiled=True),
        head_group * lane_width,
        lane_width,
        1,
    )
    running = fold_block(
        running,
        query_heads,
        piece_keys,
        piece_values,
        lax.all_gather(text_flags, "tile", axis=0, tiled=True) > 0.5,
    )
    running = fold_block(running, query_heads, own_pair[0], own_pair[1], keep_mask(0, 0, 0))
    width_set = {0: own_pair}
    for off_width in (-1, 1):
        width_set[off_width] = passed_along(own_pair, "tile", -off_width * group_count)
    width_offsets = sorted(width_set)
    row_stack = jnp.stack([width_set[spot] for spot in width_offsets])
    height_set = {0: row_stack}
    if grid_h > 1:
        for off_height in (-1, 1):
            height_set[off_height] = passed_along(
                shortened(row_stack), "tile", -off_height * grid_w * group_count
            ).astype(row_stack.dtype)
    height_offsets = sorted(height_set)
    slab_stack = jnp.stack([height_set[spot] for spot in height_offsets])

    def fold_slab(state_now, slab_pairs, off_frame):
        for h_slot, off_height in enumerate(height_offsets):
            for w_slot, off_width in enumerate(width_offsets):
                if off_frame == 0 and off_height == 0 and (off_width == 0):
                    continue
                state_now = fold_block(
                    state_now,
                    query_heads,
                    slab_pairs[h_slot, w_slot, 0],
                    slab_pairs[h_slot, w_slot, 1],
                    keep_mask(off_frame, off_height, off_width),
                )
        return state_now

    running = fold_slab(running, slab_stack, 0)
    if grid_f > 1:
        for off_frame in (-1, 1):
            got_slab = passed_along(
                shortened(slab_stack), "tile", -off_frame * grid_h * grid_w * group_count
            ).astype(slab_stack.dtype)
            running = fold_slab(running, got_slab, off_frame)
    row_top, row_total, summed = running
    result = summed / row_total[:, :, None]
    result = jnp.transpose(result, (1, 0, 2)).reshape(tokens, lane_width)
    return result.astype(jnp.bfloat16)[None]


def solution(mesh):
    return jax.shard_map(
        shards,
        mesh=mesh,
        in_specs=(
            P(("req", "tile"), None, None),
            P(("req", "tile"), None, None),
            P(("req", "tile"), None, None),
            P(("req", "tile"), None),
            P(("req", "tile"), None),
            P(("req", "tile")),
        ),
        out_specs=P(("req", "tile"), None, None),
        check_vma=False,
    )
```

profile of v0, /device:TPU:0, one launch (start us, length us, event | category | flops | bytes accessed | tf_op | source)
XLA Modules:
  0.0 110.9 jit_solution(2474602428731131896)
XLA Ops:
  0.0 0.0 copy-start.3
  0.0 0.0 copy-start.2
  0.0 0.0 copy-start
  0.0 0.0 copy-start.1
  0.0 1.2 %copy.51 = bf16[1,512,384]{1,2,0:T(8,128)(2,1)S(1)} copy(bf16[1,512,384]{2,1,0:T(8,128)(2,1)} %param.7) | data formatting | bytes 786432 | tf_op args[1]
  1.2 1.2 %copy.56 = bf16[1,512,384]{1,2,0:T(8,128)(2,1)S(1)} copy(bf16[1,512,384]{2,1,0:T(8,128)(2,1)} %param.8) | data formatting | bytes 786432 | tf_op args[2]
  2.4 1.0 fusion.71
  3.4 1.3 %collective-permute-start.1 = (bf16[2,512,384]{1,2,0:T(8,128)(2,1)}, bf16[2,512,384]{1,2,0:T(8,128)(2,1)}, u32[]{:S(2)}, u32[]{:S(2)}) collective-permute-start(bf16[2,512,384]{1,2,0:T(8,128)(2,1)} %get-tuple-element.16), channel_id=1, source_target_pairs={{4,0},{5,1},{6,2},{7,3},{8,4},{9,5},{10,6},{11,7},{12,8},{13,9},{1... | collective-permute-start | bytes 2359304 | tf_op jit(solution)/shard_map/ppermute | solution.py:16
  4.7 6.5 %collective-permute-start = (bf16[2,512,384]{1,2,0:T(8,128)(2,1)}, bf16[2,512,384]{1,2,0:T(8,128)(2,1)}, u32[]{:S(2)}, u32[]{:S(2)}) collective-permute-start(bf16[2,512,384]{1,2,0:T(8,128)(2,1)} %get-tuple-element.16), channel_id=1, source_target_pairs={{0,4},{1,5},{2,6},{3,7},{4,8},{5,9},{6,10},{7,11},{8,12},{9,13},{1... | collective-permute-start | bytes 2359304 | tf_op jit(solution)/shard_map/ppermute | solution.py:16
  11.1 0.0 copy-done.2
  11.2 0.0 copy-done.3
  11.2 0.6 dynamic-slice
  12.4 0.2 dynamic-update-slice
  12.7 41.9 %all-reduce = bf16[256]{0:T(256)(128)(2,1)S(1)} all-reduce(bf16[256]{0:T(256)(128)(2,1)S(1)} %dynamic-update-slice), channel_id=1, replica_groups=mesh['req'=2,'tile'=16] {'tile'}, use_global_device_ids=true, to_apply=%add | all-reduce | flops 256 | bytes 1024
  54.6 0.0 copy-done
  54.6 0.2 copy.46
  54.8 0.0 copy-done.1
  54.8 19.6 %all_gather.10 = bf16[256,1536]{1,0:T(8,128)(2,1)S(1)} all-gather(bf16[16,1536]{1,0:T(8,128)(2,1)S(1)} %copy-done.1), channel_id=1, replica_groups=mesh['req'=2,'tile'=16] {'tile'}, dimensions={0}, use_global_device_ids=true | all-gather | bytes 835584 | tf_op jit(solution)/shard_map/all_gather | solution.py:80
  74.4 21.4 %all_gather.11 = bf16[256,1536]{1,0:T(8,128)(2,1)S(1)} all-gather(bf16[16,1536]{1,0:T(8,128)(2,1)} %param.10), channel_id=1, replica_groups=mesh['req'=2,'tile'=16] {'tile'}, dimensions={0}, use_global_device_ids=true | all-gather | bytes 835584 | tf_op jit(solution)/shard_map/all_gather | solution.py:86
  95.8 0.8 constant_dynamic-slice_fusion
  96.6 1.1 copy.49
  97.6 1.1 copy.79
  98.8 0.4 bitcast_reduce_fusion.2
  99.2 0.8 fusion.4
  100.0 0.0 collective-permute-done.1
  100.0 0.0 collective-permute-done
  100.0 1.6 %maximum_bitcast_fusion = bf16[1,3,2,512,384]{3,4,2,1,0:T(8,128)(2,1)S(1)} fusion(bf16[1,2,512,384]{2,3,1,0:T(8,128)(2,1)} %bitcast.13, bf16[1,2,512,384]{2,3,1,0:T(8,128)(2,1)S(1)} %get-tuple-element.15, bf16[1,2,512,384]{2,3,1,0:T(8,128)(2,1)} %bitcast.11), kind=kLoop, calls=%fused_computation.13 | loop fusion | flops 2359296 | bytes 4718592 | tf_op jit(solution)/shard_map/stack | solution.py:111
  101.7 0.1 fusion.75
  101.8 0.8 bitcast_reduce_fusion
  102.6 0.8 bitcast_reduce_fusion.1
  103.5 0.9 fusion.9
  104.3 1.0 fusion.38
  105.3 0.9 fusion.7
  106.2 1.0 fusion.35
  107.2 0.9 fusion.5
  108.1 1.0 fusion.24
  109.1 0.3 fusion.41
  109.4 0.6 fusion.43
  110.0 0.9 copy.66
  (7 shorter events, 0.1 us)
Async XLA Ops:
  0.0 11.2 %copy-start.3 = (u32[32]{0:T(128)S(1)}, u32[32]{0:T(128)}, u32[]{:S(2)}) copy-start(u32[32]{0:T(128)} %constant.104) | copy-start | bytes 388
  0.0 11.1 %copy-start.2 = (s32[16]{0:T(128)S(1)}, s32[16]{0:T(128)}, u32[]{:S(2)}) copy-start(s32[16]{0:T(128)} %param.11) | copy-start | bytes 196
  0.0 54.6 %copy-start = (bf16[1,512,384]{2,1,0:T(8,128)(2,1)S(1)}, bf16[1,512,384]{2,1,0:T(8,128)(2,1)}, u32[]{:S(2)}) copy-start(bf16[1,512,384]{2,1,0:T(8,128)(2,1)} %param.6) | copy-start | bytes 1179652
  0.0 54.8 %copy-start.1 = (bf16[16,1536]{1,0:T(8,128)(2,1)S(1)}, bf16[16,1536]{1,0:T(8,128)(2,1)}, u32[]{:S(2)}) copy-start(bf16[16,1536]{1,0:T(8,128)(2,1)} %param.9) | copy-start | bytes 147460
  3.4 96.6 %collective-permute-start.1 = (bf16[2,512,384]{1,2,0:T(8,128)(2,1)}, bf16[2,512,384]{1,2,0:T(8,128)(2,1)}, u32[]{:S(2)}, u32[]{:S(2)}) collective-permute-start(bf16[2,512,384]{1,2,0:T(8,128)(2,1)} %get-tuple-element.16), channel_id=1, source_target_pairs={{4,0},{5,1},{6,2},{7,3},{8,4},{9,5},{10,6},{11,7},{12,8},{13,9},{1... | collective-permute-start | bytes 2359304 | tf_op jit(solution)/shard_map/ppermute | solution.py:16
  4.7 95.4 %collective-permute-start = (bf16[2,512,384]{1,2,0:T(8,128)(2,1)}, bf16[2,512,384]{1,2,0:T(8,128)(2,1)}, u32[]{:S(2)}, u32[]{:S(2)}) collective-permute-start(bf16[2,512,384]{1,2,0:T(8,128)(2,1)} %get-tuple-element.16), channel_id=1, source_target_pairs={{0,4},{1,5},{2,6},{3,7},{4,8},{5,9},{6,10},{7,11},{8,12},{9,13},{1... | collective-permute-start | bytes 2359304 | tf_op jit(solution)/shard_map/ppermute | solution.py:16
where the time goes:
time: 111 us
  blocking collectives  82.9 us (75%)
  starting transfers between devices  7.75 us (7%)
  local copies, waits for them, and re-layouts  7.34 us (7%)
  matrix products  6.38 us (6%)
  other arithmetic  5.66 us (5%)
    unnamed x1, blocking collectives  41.9 us
    all_gather x1, blocking collectives, shards(): lax.all_gather(text_values, 'tile', axis=0, tiled=True)  21.4 us
    all_gather x1, blocking collectives, shards(): lax.all_gather(text_keys, 'tile', axis=0, tiled=True)  19.6 us
    ppermute x2, starting transfers between devices, passed_along(): lax.ppermute(value, axis, [(source, source + steps) for source in range(f...  7.75 us
    unnamed x15, local copies, waits for them, and re-layouts  4.48 us
    dot_general x4, matrix products, fold_block(): jnp.einsum('hqk,khd->hqd', weights, value_heads, preferred_element_type=j...  3.48 us
    reduce_sum x4, other arithmetic, fold_block(): row_total = row_total * scale_down + jnp.sum(exp_terms, axis=-1)  2.97 us
    dot_general x4, matrix products, fold_block(): jnp.einsum('qhd,khd->hqk', query_heads, key_heads, preferred_element_type...  2.9 us
  transfers between devices with their start and end apart: 2, of which 0 were waited for; matrix products, arithmetic and copies ran while one was open for 5% of the time, Pallas kernels for 0%

commit v1 on v0

--- a/solution.py
+++ b/solution.py
@@ -8,6 +8,18 @@
 HEAD_DIM = 128
 HEAD_GROUPS = 4
 MASKED = -1e30
+
+
+def collect(x, axis, dim):
+    ways, here, step = (lax.axis_size(axis), lax.axis_index(axis), x.shape[dim])
+    line, have = (x, 1)
+    while have < ways:
+        line = jnp.concatenate(
+            [line, lax.ppermute(line, axis, [(d, (d - have) % ways) for d in range(ways)])],
+            axis=dim,
+        )
+        have = 2 * have
+    return jnp.roll(line, here * step, axis=dim)
 
 
 def passed_along(value, axis, steps):
@@ -77,10 +89,7 @@
     )
     text_flags = text_mask.astype(jnp.bfloat16)
     piece_keys = lax.dynamic_slice_in_dim(
-        lax.all_gather(text_keys, "tile", axis=0, tiled=True),
-        head_group * lane_width,
-        lane_width,
-        1,
+        collect(text_keys, "tile", 0), head_group * lane_width, lane_width, 1
     )
     piece_values = lax.dynamic_slice_in_dim(
         lax.all_gather(text_values, "tile", axis=0, tiled=True),

time: 111 us -> 143 us (1.29)
  waiting for transfers between devices: 0.01 us -> 36.4 us
  blocking collectives: 82.9 us -> 64.6 us
  local copies, waits for them, and re-layouts: 7.34 us -> 13.3 us
  starting transfers between devices: 7.75 us -> 12 us
  other arithmetic: 5.66 us -> 7.93 us
    ppermute x0 -> x4, waiting for transfers between devices: none -> 36.4 us  [collect(): lax.ppermute(line, axis, [(d, (d - have) % ways) for d in range(ways)])]
    all_gather x1 -> x0, blocking collectives: 19.6 us -> none  [shards(): lax.all_gather(text_keys, 'tile', axis=0, tiled=True)]
    all_gather x1, blocking collectives: 21.4 us -> 34.8 us  [shards(): lax.all_gather(text_values, 'tile', axis=0, tiled=True)]
    unnamed x1, blocking collectives: 41.9 us -> 29.8 us
    concatenate x0 -> x1, local copies, waits for them, and re-layouts: none -> 5.62 us  [collect(): return jnp.roll(line, here * step, axis=dim)]
    ppermute x0 -> x4, starting transfers between devices: none -> 4.93 us  [collect(): lax.ppermute(line, axis, [(d, (d - have) % ways) for d in range(ways)])]
    unnamed x15 -> x43, local copies, waits for them, and re-layouts: 4.48 us -> 4.73 us
  transfers between devices with their start and end apart: 2 -> 6, of which waited for: 0 -> 3; matrix products, arithmetic and copies ran while one was open for 5% -> 9% of each run, Pallas kernels for 0% -> 0%
where the time goes in v1:
time: 143 us
  blocking collectives  64.6 us (45%)
  waiting for transfers between devices  36.4 us (25%)
  local copies, waits for them, and re-layouts  13.3 us (9%)
  starting transfers between devices  12 us (8%)
  other arithmetic  7.93 us (6%)
  matrix products  7.36 us (5%)
    ppermute x4, waiting for transfers between devices, collect(): lax.ppermute(line, axis, [(d, (d - have) % ways) for d in range(ways)])  36.4 us
    all_gather x1, blocking collectives, shards(): lax.all_gather(text_values, 'tile', axis=0, tiled=True)  34.8 us
    unnamed x1, blocking collectives  29.8 us
    ppermute x2, starting transfers between devices, passed_along(): lax.ppermute(value, axis, [(source, source + steps) for source in range(f...  7.11 us
    concatenate x1, local copies, waits for them, and re-layouts, collect(): return jnp.roll(line, here * step, axis=dim)  5.62 us
    ppermute x4, starting transfers between devices, collect(): lax.ppermute(line, axis, [(d, (d - have) % ways) for d in range(ways)])  4.93 us
    unnamed x43, local copies, waits for them, and re-layouts  4.73 us
    dot_general x4, matrix products, fold_block(): jnp.einsum('qhd,khd->hqk', query_heads, key_heads, preferred_element_type...  3.89 us
  transfers between devices with their start and end apart: 6, of which 3 were waited for; matrix products, arithmetic and copies ran while one was open for 9% of the time, Pallas kernels for 0%

profile of v1, /device:TPU:0, one launch (start us, length us, event | category | flops | bytes accessed | tf_op | source)
XLA Modules:
  0.0 142.7 jit_solution(7738860658897163337)
XLA Ops:
  0.0 1.2 copy.89
  1.2 0.0 copy-start.17
  1.3 1.3 copy.94
  2.6 1.3 fusion.71
  3.9 5.8 %collective-permute-start.4 = (bf16[2,512,384]{1,2,0:T(8,128)(2,1)}, bf16[2,512,384]{1,2,0:T(8,128)(2,1)}, u32[]{:S(2)}, u32[]{:S(2)}) collective-permute-start(bf16[2,512,384]{1,2,0:T(8,128)(2,1)} %get-tuple-element.16), channel_id=1, source_target_pairs={{0,4},{1,5},{2,6},{3,7},{4,8},{5,9},{6,10},{7,11},{8,12},{9,13},{1... | collective-permute-start | bytes 2359304 | tf_op jit(solution)/shard_map/ppermute | solution.py:28
  9.7 1.3 collective-permute-start.5
  11.0 0.0 copy-done.11
  11.0 0.2 copy.82
  11.2 4.6 %collective-permute-start = (bf16[16,1536]{0,1:T(8,128)(2,1)S(1)}, bf16[16,1536]{0,1:T(8,128)(2,1)S(1)}, u32[]{:S(2)}, u32[]{:S(2)}) collective-permute-start(bf16[16,1536]{0,1:T(8,128)(2,1)S(1)} %copy.82), channel_id=1, source_target_pairs={{0,15},{1,0},{2,1},{3,2},{4,3},{5,4},{6,5},{7,6},{8,7},{9,8},{10,9... | collective-permute-start | bytes 147464 | tf_op jit(solution)/shard_map/ppermute | solution.py:18
  15.8 34.8 %all_gather.7 = bf16[256,1536]{1,0:T(8,128)(2,1)S(1)} all-gather(bf16[16,1536]{1,0:T(8,128)(2,1)S(1)} %copy-done.12), channel_id=1, replica_groups=mesh['req'=2,'tile'=16] {'tile'}, dimensions={0}, use_global_device_ids=true | all-gather | bytes 835584 | tf_op jit(solution)/shard_map/all_gather | solution.py:95
  50.7 0.9 copy.84
  51.7 0.8 copy.87
  52.5 0.6 dynamic-slice
  53.7 0.2 dynamic-update-slice
  54.0 29.8 %all-reduce = bf16[256]{0:T(256)(128)(2,1)S(1)} all-reduce(bf16[256]{0:T(256)(128)(2,1)S(1)} %dynamic-update-slice), channel_id=1, replica_groups=mesh['req'=2,'tile'=16] {'tile'}, use_global_device_ids=true, to_apply=%add | all-reduce | flops 256 | bytes 1024
  83.8 0.0 collective-permute-done
  83.9 0.2 pad_maximum_fusion.1
  84.1 0.0 copy-done.4
  84.1 0.1 collective-permute-start.1
  84.2 10.5 %collective-permute-done.1 = bf16[32,1536]{0,1:T(8,128)(2,1)S(1)} collective-permute-done((bf16[32,1536]{0,1:T(8,128)(2,1)S(1)}, bf16[32,1536]{0,1:T(8,128)(2,1)S(1)}, u32[]{:S(2)}, u32[]{:S(2)}) %collective-permute-start.1) | collective-permute-done | bytes 98336 | tf_op jit(solution)/shard_map/ppermute | solution.py:18
  94.7 0.4 pad_maximum_fusion.2
  95.1 0.2 collective-permute-start.2
  95.3 0.6 broadcast_compare_fusion
  95.9 9.0 %collective-permute-done.2 = bf16[64,1536]{0,1:T(8,128)(2,1)S(1)} collective-permute-done((bf16[64,1536]{0,1:T(8,128)(2,1)S(1)}, bf16[64,1536]{0,1:T(8,128)(2,1)S(1)}, u32[]{:S(2)}, u32[]{:S(2)}) %collective-permute-start.2) | collective-permute-done | bytes 196640 | tf_op jit(solution)/shard_map/ppermute | solution.py:18
  104.9 0.5 pad_maximum_fusion.3
  105.4 0.1 collective-permute-start.3
  105.6 0.1 copy-done.6
  105.7 0.8 fusion.4
  106.5 16.9 %collective-permute-done.3 = bf16[128,1536]{0,1:T(8,128)(2,1)} collective-permute-done((bf16[128,1536]{0,1:T(8,128)(2,1)S(1)}, bf16[128,1536]{0,1:T(8,128)(2,1)}, u32[]{:S(2)}, u32[]{:S(2)}) %collective-permute-start.3) | collective-permute-done | bytes 393248 | tf_op jit(solution)/shard_map/ppermute | solution.py:18
  123.4 5.6 %concatenate.21 = bf16[512,1536]{0,1:T(8,128)(2,1)} concatenate(bf16[16,1536]{0,1:T(8,128)(2,1)S(1)} %copy.82, bf16[16,1536]{0,1:T(8,128)(2,1)} %copy-done.2, bf16[32,1536]{0,1:T(8,128)(2,1)} %copy-done.3, bf16[64,1536]{0,1:T(8,128)(2,1)} %copy-done.6, bf16[128,1536]{0,1:T(8,128)(2,1)} %collective-permute-done.3, bf16[16,1536]{0,1:T(8,128)(2,1)S(1)} %copy.82, ...), dimensions={0} | concatenate | bytes 3145728 | tf_op jit(solution)/shard_map/jit(_roll_dynamic)/concatenate | solution.py:22
  129.0 1.1 dynamic_slice.8
  130.1 1.4 %bitcast_reduce_fusion.2 = (f32[3,512]{1,0:T(4,128)S(1)}, f32[3,256,512]{2,1,0:T(8,128)S(1)}) fusion(bf16[256,3,128]{0,2,1:T(8,128)(2,1)S(1)} %bitcast.168, bf16[512,3,128]{0,2,1:T(8,128)(2,1)} %bitcast.160, pred[256]{0:T(512)(128)(4,1)} %broadcast_compare_fusion), kind=kOutput, calls=%fused_computation.21 | convolution fusion | flops 101841408 | bytes 2169088 | tf_op jit(solution)/shard_map/qhd,khd->hqk/dot_general | solution.py:40
  131.5 0.0 collective-permute-done.4
  131.5 0.0 collective-permute-done.5
  131.5 0.0 copy-start.1
  131.5 1.9 %maximum_bitcast_fusion = bf16[1,3,2,512,384]{3,4,2,1,0:T(8,128)(2,1)S(1)} fusion(bf16[1,2,512,384]{2,3,1,0:T(8,128)(2,1)} %bitcast.13, bf16[1,2,512,384]{2,3,1,0:T(8,128)(2,1)} %get-tuple-element.15, bf16[1,2,512,384]{2,3,1,0:T(8,128)(2,1)} %bitcast.11), kind=kLoop, calls=%fused_computation.13 | loop fusion | flops 2359296 | bytes 4718592 | tf_op jit(solution)/shard_map/stack | solution.py:120
  133.4 0.1 fusion.75
  133.6 0.8 bitcast_reduce_fusion.1
  134.4 0.8 bitcast_reduce_fusion
  135.3 0.9 fusion.5
  136.2 1.0 fusion.24
  137.1 0.9 fusion.7
  138.0 1.0 fusion.35
  139.0 0.9 fusion.9
  139.9 1.0 fusion.38
  140.9 0.3 fusion.41
  141.2 0.6 fusion.43
  141.8 0.9 copy.104
  (38 shorter events, 0.2 us)
Async XLA Ops:
  0.0 11.0 %copy-start.11 = (bf16[16,1536]{1,0:T(8,128)(2,1)S(1)}, bf16[16,1536]{1,0:T(8,128)(2,1)}, u32[]{:S(2)}) copy-start(bf16[16,1536]{1,0:T(8,128)(2,1)} %param.9) | copy-start | bytes 147460
  0.0 15.8 %copy-start.12 = (bf16[16,1536]{1,0:T(8,128)(2,1)S(1)}, bf16[16,1536]{1,0:T(8,128)(2,1)}, u32[]{:S(2)}) copy-start(bf16[16,1536]{1,0:T(8,128)(2,1)} %param.10) | copy-start | bytes 147460
  0.0 50.7 %copy-start.9 = (bf16[1,512,384]{2,1,0:T(8,128)(2,1)S(1)}, bf16[1,512,384]{2,1,0:T(8,128)(2,1)}, u32[]{:S(2)}) copy-start(bf16[1,512,384]{2,1,0:T(8,128)(2,1)} %param.6) | copy-start | bytes 1179652
  0.0 51.6 %copy-start.16 = (s32[16]{0:T(128)S(1)}, s32[16]{0:T(128)}, u32[]{:S(2)}) copy-start(s32[16]{0:T(128)} %param.11) | copy-start | bytes 196
  1.2 82.9 %copy-start.4 = (bf16[1,512,384]{1,2,0:T(8,128)(2,1)}, bf16[1,512,384]{1,2,0:T(8,128)(2,1)S(1)}, u32[]{:S(2)}) copy-start(bf16[1,512,384]{1,2,0:T(8,128)(2,1)S(1)} %copy.89) | copy-start | bytes 1179652
  1.2 51.2 %copy-start.17 = (u32[32]{0:T(128)S(1)}, u32[32]{0:T(128)}, u32[]{:S(2)}) copy-start(u32[32]{0:T(128)} %constant.138) | copy-start | bytes 388
  2.6 7.1 %copy-start.7 = (bf16[1,512,384]{1,2,0:T(8,128)(2,1)}, bf16[1,512,384]{1,2,0:T(8,128)(2,1)S(1)}, u32[]{:S(2)}) copy-start(bf16[1,512,384]{1,2,0:T(8,128)(2,1)S(1)} %copy.94) | copy-start | bytes 1179652
  3.9 127.6 %collective-permute-start.4 = (bf16[2,512,384]{1,2,0:T(8,128)(2,1)}, bf16[2,512,384]{1,2,0:T(8,128)(2,1)}, u32[]{:S(2)}, u32[]{:S(2)}) collective-permute-start(bf16[2,512,384]{1,2,0:T(8,128)(2,1)} %get-tuple-element.16), channel_id=1, source_target_pairs={{0,4},{1,5},{2,6},{3,7},{4,8},{5,9},{6,10},{7,11},{8,12},{9,13},{1... | collective-permute-start | bytes 2359304 | tf_op jit(solution)/shard_map/ppermute | solution.py:28
  9.7 121.8 %collective-permute-start.5 = (bf16[2,512,384]{1,2,0:T(8,128)(2,1)}, bf16[2,512,384]{1,2,0:T(8,128)(2,1)}, u32[]{:S(2)}, u32[]{:S(2)}) collective-permute-start(bf16[2,512,384]{1,2,0:T(8,128)(2,1)} %get-tuple-element.16), channel_id=1, source_target_pairs={{4,0},{5,1},{6,2},{7,3},{8,4},{9,5},{10,6},{11,7},{12,8},{13,9},{1... | collective-permute-start | bytes 2359304 | tf_op jit(solution)/shard_map/ppermute | solution.py:28
  11.2 72.6 %collective-permute-start = (bf16[16,1536]{0,1:T(8,128)(2,1)S(1)}, bf16[16,1536]{0,1:T(8,128)(2,1)S(1)}, u32[]{:S(2)}, u32[]{:S(2)}) collective-permute-start(bf16[16,1536]{0,1:T(8,128)(2,1)S(1)} %copy.82), channel_id=1, source_target_pairs={{0,15},{1,0},{2,1},{3,2},{4,3},{5,4},{6,5},{7,6},{8,7},{9,8},{10,9... | collective-permute-start | bytes 147464 | tf_op jit(solution)/shard_map/ppermute | solution.py:18
  83.8 21.8 %copy-start = (bf16[1,512,384]{1,2,0:T(8,128)(2,1)S(1)}, bf16[1,512,384]{1,2,0:T(8,128)(2,1)}, u32[]{:S(2)}) copy-start(bf16[1,512,384]{1,2,0:T(8,128)(2,1)} %copy.84) | copy-start | bytes 1179652
  83.8 21.7 %copy-start.2 = (bf16[16,1536]{0,1:T(8,128)(2,1)}, bf16[16,1536]{0,1:T(8,128)(2,1)S(1)}, u32[]{:S(2)}) copy-start(bf16[16,1536]{0,1:T(8,128)(2,1)S(1)} %collective-permute-done) | copy-start | bytes 147460
  84.1 10.6 %collective-permute-start.1 = (bf16[32,1536]{0,1:T(8,128)(2,1)S(1)}, bf16[32,1536]{0,1:T(8,128)(2,1)S(1)}, u32[]{:S(2)}, u32[]{:S(2)}) collective-permute-start(bf16[32,1536]{0,1:T(8,128)(2,1)S(1)} %pad_maximum_fusion.1), channel_id=1, source_target_pairs={{0,14},{1,15},{2,0},{3,1},{4,2},{5,3},{6,4},{7,5},{8,6},{9,7},{10,... | collective-permute-start | bytes 294920 | tf_op jit(solution)/shard_map/ppermute | solution.py:18
  84.2 21.5 %copy-start.5 = (bf16[1,512,384]{1,2,0:T(8,128)(2,1)S(1)}, bf16[1,512,384]{1,2,0:T(8,128)(2,1)}, u32[]{:S(2)}) copy-start(bf16[1,512,384]{1,2,0:T(8,128)(2,1)} %copy-done.4) | copy-start | bytes 1179652
  94.7 10.9 %copy-start.3 = (bf16[32,1536]{0,1:T(8,128)(2,1)}, bf16[32,1536]{0,1:T(8,128)(2,1)S(1)}, u32[]{:S(2)}) copy-start(bf16[32,1536]{0,1:T(8,128)(2,1)S(1)} %collective-permute-done.1) | copy-start | bytes 294916
  95.1 9.9 %collective-permute-start.2 = (bf16[64,1536]{0,1:T(8,128)(2,1)S(1)}, bf16[64,1536]{0,1:T(8,128)(2,1)S(1)}, u32[]{:S(2)}, u32[]{:S(2)}) collective-permute-start(bf16[64,1536]{0,1:T(8,128)(2,1)S(1)} %pad_maximum_fusion.2), channel_id=1, source_target_pairs={{0,12},{1,13},{2,14},{3,15},{4,0},{5,1},{6,2},{7,3},{8,4},{9,5},{1... | collective-permute-start | bytes 589832 | tf_op jit(solution)/shard_map/ppermute | solution.py:18
  104.9 0.8 copy-start.6
  105.4 17.9 %collective-permute-start.3 = (bf16[128,1536]{0,1:T(8,128)(2,1)S(1)}, bf16[128,1536]{0,1:T(8,128)(2,1)}, u32[]{:S(2)}, u32[]{:S(2)}) collective-permute-start(bf16[128,1536]{0,1:T(8,128)(2,1)S(1)} %pad_maximum_fusion.3), channel_id=1, source_target_pairs={{0,8},{1,9},{2,10},{3,11},{4,12},{5,13},{6,14},{7,15},{8,0},{9,1},... | collective-permute-start | bytes 1179656 | tf_op jit(solution)/shard_map/ppermute | solution.py:18
  105.5 1.0 copy-start.14
  131.5 2.0 %copy-start.1 = (bf16[1,512,384]{1,2,0:T(8,128)(2,1)S(1)}, bf16[1,512,384]{1,2,0:T(8,128)(2,1)}, u32[]{:S(2)}) copy-start(bf16[1,512,384]{1,2,0:T(8,128)(2,1)} %copy.84) | copy-start | bytes 1179652
  133.6 1.7 %copy-start.15 = (pred[512]{0:T(512)(128)(4,1)S(1)}, pred[512]{0:T(512)(128)(4,1)}, u32[]{:S(2)}) copy-start(pred[512]{0:T(512)(128)(4,1)} %copy-done.14) | copy-start | bytes 1540
  134.4 1.8 %copy-start.8 = (bf16[1,512,384]{1,2,0:T(8,128)(2,1)S(1)}, bf16[1,512,384]{1,2,0:T(8,128)(2,1)}, u32[]{:S(2)}) copy-start(bf16[1,512,384]{1,2,0:T(8,128)(2,1)} %copy-done.7) | copy-start | bytes 1179652
  139.9 1.0 copy-start.13
  139.9 1.4 copy-start.10
